TPU v7x, 32 devices: a whole 2x2x4 slice. The times are simulated.
32 devices in a mesh: space: 8 (over y, x, core), species: 4 (over z).
Axes of the slice: x: 2, y: 2, z: 4, core: 2. Of those that a mesh axis runs over, the one named last changes fastest.
Arguments:
- cotangent: bfloat16 [4, 400, 20, 1024], P('species', None, None, 'space'), may hold values from -6 to 6
- freq: float32 [4], P('species'), may hold values from 0.2 to 0.9
- ratio: float32 [4], P('species'), may hold values from 0.5 to 1
- coupling: float32 [4, 4, 13], replicated, may hold values from 0.1 to 0.6
- wall: int32 [1024], P('space'), may hold values 0 or 1
- inlet: int32 [1024], P('space'), may hold values 0 or 1
- face_type: int32 [2, 8], P(None, 'space'), may hold values from 0 to 1
Outputs:
- grad_state: bfloat16 [4, 400, 20, 1024], P('species', None, None, 'space')
Inputs may be any that keep to these rules, and one draw needn't show every extreme that they name: `wall`: 1 marks a solid cell. `inlet`: 1 marks an inlet cell. `face_type`: 0 is a specular wall, 1 a reversing wall.
All inputs are finite; a program needn't handle non-finite values. No bound on the sum of `wall` or of `inlet` on one device may be relied on, other than what follows from the above.
Results may differ from a plain program's by a relative error of at most 0.0049.
Values may be sent and summed in bfloat16 or wider, within the bound.
No kernel may reach another device: no remote copies, remote signals or barrier semaphores. Data moves between devices by JAX's collectives and lax.ppermute only.
A program may use at most 64 MiB of HBM per device.

v0:
```python
import math

import jax
import jax.numpy as jnp
from jax import lax
from jax.sharding import PartitionSpec as P

NZ = 128


courant_max = 0.45
node_reach = 2.85


def passed_along(value, axis, steps):
    count = lax.axis_size(axis)
    pairs = [(source, (source + steps) % count) for source in range(count)]
    return lax.ppermute(value, axis, pairs)


def velocity_tables(node_count):
    pair_count = node_count * node_count
    spacing = 2.0 * node_reach / (node_count - 1)
    node_line = (
        jnp.arange(node_count, dtype=jnp.int32).astype(jnp.float32) - 0.5 * (node_count - 1)
    ) * spacing
    grid_shape = (pair_count, node_count)
    along_x = jnp.broadcast_to(jnp.repeat(node_line, node_count)[:, None], grid_shape)
    along_y = jnp.broadcast_to(jnp.tile(node_line, node_count)[:, None], grid_shape)
    along_z = jnp.broadcast_to(node_line[None, :], grid_shape)
    square = along_x * along_x + along_y * along_y + along_z * along_z
    heat_term = square - 2.5
    functions = [
        jnp.ones(grid_shape, jnp.float32),
        along_x,
        along_y,
        along_z,
        square - 1.5,
        along_x * along_y,
        along_x * along_z,
        along_y * along_z,
        along_x * along_x - along_y * along_y,
        along_y * along_y - along_z * along_z,
        along_x * heat_term,
        along_y * heat_term,
        along_z * heat_term,
    ]
    stacked = jnp.stack(functions).reshape(len(functions), pair_count * node_count)
    basis_table = stacked / jnp.sqrt(jnp.mean(stacked * stacked, axis=1, keepdims=True))
    weights = jnp.exp(-square).reshape(-1) * (spacing * spacing * spacing) / math.pi**1.5
    recon_table = basis_table * weights[None, :]
    return (node_line, basis_table, recon_table)


def keep_factor(wall, inlet, pair_count):
    upward = (jnp.arange(pair_count, dtype=jnp.int32) >= pair_count // 2).astype(jnp.float32)
    open_cells = (1 - wall).astype(jnp.float32)
    inflow = inlet.astype(jnp.float32)
    return open_cells[None, None, :] * (1.0 - upward[:, None, None] * inflow[None, None, :])


def on_device(cotangent, freq, ratio, coupling, wall, inlet, face_type):
    pair_count = cotangent.shape[1]
    node_count = cotangent.shape[2]
    cell_count = cotangent.shape[3]
    depth_cells = NZ
    column_count = cell_count // depth_cells
    half_pairs = pair_count // 2
    node_line, basis_table, recon_table = velocity_tables(node_count)
    keep_mask = keep_factor(wall, inlet, pair_count)
    masked = cotangent[0] * keep_mask.astype(jnp.bfloat16)
    moments = jnp.dot(
        basis_table,
        masked.reshape(pair_count * node_count, cell_count),
        precision=lax.Precision.HIGHEST,
        preferred_element_type=jnp.float32,
    )
    species_index = lax.axis_index("species")
    rate_value = freq[0]
    row_k = lax.dynamic_index_in_dim(coupling, species_index, axis=0, keepdims=False)
    cross_terms = jnp.sum(
        row_k[:, :, None] * lax.all_gather(moments[None], "species", axis=0, tiled=True), axis=0
    )
    rebuilt = jnp.dot(
        recon_table.T,
        cross_terms,
        precision=lax.Precision.HIGHEST,
        preferred_element_type=jnp.float32,
    ).reshape(pair_count, node_count, cell_count)
    relaxed = ((1.0 - rate_value) * masked.astype(jnp.float32) + rebuilt).astype(jnp.bfloat16)
    rim_shape = (half_pairs, node_count, depth_cells)
    zero_half = jnp.zeros(rim_shape, jnp.bfloat16)
    first_upper = relaxed[half_pairs:, :, :depth_cells].reshape(
        half_pairs, node_count * depth_cells
    )
    got_next = passed_along(first_upper, "space", -1).reshape(rim_shape)
    last_lower = relaxed[:half_pairs, :, cell_count - depth_cells :].reshape(
        half_pairs, node_count * depth_cells
    )
    got_prev = passed_along(last_lower, "space", 1).reshape(rim_shape)
    next_rim = jnp.concatenate([zero_half, got_next], axis=0)
    prev_rim = jnp.concatenate([got_prev, zero_half], axis=0)
    field = relaxed.astype(jnp.float32).reshape(pair_count, node_count, column_count, depth_cells)
    scale_factor = courant_max * ratio[0] / node_reach
    adv_x = (scale_factor * jnp.repeat(node_line, node_count))[:, None, None, None]
    adv_z = (scale_factor * node_line)[None, :, None, None]
    plus_x = jnp.maximum(adv_x, 0.0)
    minus_x = jnp.maximum(-adv_x, 0.0)
    plus_z = jnp.maximum(adv_z, 0.0)
    minus_z = jnp.maximum(-adv_z, 0.0)
    shifted_up_x = jnp.concatenate(
        [field[:, :, 1:], next_rim.astype(jnp.float32)[:, :, None, :]], axis=2
    )
    shifted_down_x = jnp.concatenate(
        [prev_rim.astype(jnp.float32)[:, :, None, :], field[:, :, : column_count - 1]], axis=2
    )
    zero_plane = jnp.zeros_like(field[..., :1])
    upper_z = jnp.concatenate([field[..., 1:], zero_plane], axis=3)
    lower_z = jnp.concatenate([zero_plane, field[..., :-1]], axis=3)
    result = (1.0 - jnp.abs(adv_x) - jnp.abs(adv_z)) * field
    result = result + plus_x * shifted_up_x + minus_x * shifted_down_x
    result = result + plus_z * upper_z + minus_z * lower_z
    bottom_part = plus_z[..., 0] * field[..., 0]
    bottom_add = jnp.where(
        face_type[0][None, None, :] == 1,
        jnp.flip(bottom_part, axis=(0, 1)),
        jnp.flip(bottom_part, axis=1),
    )
    top_part = minus_z[..., 0] * field[..., depth_cells - 1]
    top_add = jnp.where(
        face_type[1][None, None, :] == 1,
        jnp.flip(top_part, axis=(0, 1)),
        jnp.flip(top_part, axis=1),
    )
    result = result.at[..., 0].add(bottom_add)
    result = result.at[..., depth_cells - 1].add(top_add)
    return result.reshape(pair_count, node_count, cell_count).astype(jnp.bfloat16)[None]


def solution(mesh):
    in_specs = (
        P("species", None, None, "space"),
        P("species"),
        P("species"),
        P(),
        P("space"),
        P("space"),
        P(None, "space"),
    )
    out_specs = P("species", None, None, "space")
    return jax.shard_map(
        on_device, mesh=mesh, in_specs=in_specs, out_specs=out_specs, check_vma=False
    )
```

profile of v0, /device:TPU:0, one launch (start us, length us, event | category | flops | bytes accessed | tf_op | source)
XLA Modules:
  0.0 107.0 jit_solution(7815667221158033408)
XLA Ops:
  1.0 0.1 exponential_multiply_fusion
  1.1 0.1 div.31
  1.4 0.2 stack_broadcast_in_dim.58
  1.7 0.2 stack_broadcast_in_dim.61
  1.9 0.2 stack_broadcast_in_dim.63
  2.2 0.2 broadcast_in_dim.135
  2.5 0.2 broadcast_in_dim.129
  2.7 0.2 broadcast_in_dim.131
  3.0 0.2 broadcast_in_dim.137
  3.3 0.2 broadcast_in_dim.133
  3.6 0.2 stack.21
  3.9 0.2 stack.23
  4.4 0.6 stack.24
  5.0 0.2 multiply_reduce_fusion
  5.2 0.9 multiply_bitcast_fusion
  6.1 2.8 %dot_general.11 = f32[400,20,13]{1,0,2:T(8,128)S(1)} reshape(f32[8000,13]{0,1:T(8,128)} %multiply_bitcast_fusion) | data formatting | bytes 832000 | tf_op jit(solution)/shard_map/dot_general | solution.py:84
  9.0 2.7 %copy.47 = f32[400,20,13]{0,2,1:T(8,128)} copy(f32[400,20,13]{1,0,2:T(8,128)S(1)} %dot_general.11) | data formatting | bytes 832000 | tf_op jit(solution)/shard_map/dot_general | solution.py:84
  12.4 2.2 %copy.45 = bf16[1,400,20,128]{3,2,1,0:T(8,128)(2,1)S(1)} copy(bf16[1,400,20,128]{3,1,2,0:T(8,128)(2,1)} %param.11) | data formatting | bytes 4096000 | tf_op args[0]
  14.5 2.0 %squeeze.18 = bf16[8000,128]{1,0:T(8,128)(2,1)} reshape(bf16[1,400,20,128]{3,2,1,0:T(8,128)(2,1)S(1)} %copy.45) | data formatting | bytes 4096000 | tf_op jit(solution)/shard_map/squeeze | solution.py:71
  16.6 0.3 mul.346.clone
  17.0 2.0 %mul.363 = bf16[8000,128]{1,0:T(8,128)(2,1)} reshape(bf16[400,20,128]{2,1,0:T(8,128)(2,1)S(1)} %mul.346.clone) | data formatting | bytes 4096000 | tf_op jit(solution)/shard_map/mul | solution.py:71
  19.0 3.3 %fusion.8 = f32[1,13,128]{2,1,0:T(8,128)S(1)} fusion(bf16[8000,128]{1,0:T(8,128)(2,1)} %squeeze.18, bf16[8000,128]{1,0:T(8,128)(2,1)} %mul.363, f32[13,8000]{1,0:T(8,128)S(1)} %stack.24, f32[13]{0:T(128)S(1)} %multiply_sqrt_fusion), kind=kOutput, calls=%fused_computation.17 | convolution fusion | flops 160872000 | bytes 4518708 | tf_op jit(solution)/shard_map/dot_general | solution.py:72
  22.3 14.9 %all-gather.1 = f32[4,13,128]{2,1,0:T(8,128)S(1)} all-gather(f32[1,13,128]{2,1,0:T(8,128)S(1)} %fusion.8), channel_id=2, replica_groups=mesh['space'=8,'species'=4] {'species'}, dimensions={0}, use_global_device_ids=true | all-gather | bytes 33280 | tf_op jit(solution)/shard_map/all_gather | solution.py:82
  37.2 8.1 %add_convert_fusion = bf16[400,20,128]{2,0,1:T(8,128)(2,1)S(1)} fusion(f32[400,20,13]{0,2,1:T(8,128)} %copy.47, bf16[1,400,20,128]{3,1,2,0:T(8,128)(2,1)} %param.11, f32[]{:T(128)} %bitcast.2, bf16[400,128]{1,0:T(8,128)(2,1)S(1)} %multiply_convert_fusion, f32[13,128]{1,0:T(8,128)S(1)} %multiply_reduce_fusion.1), kind=kOutput, calls=%fused_computation.12 | convolution fusion | flops 164864000 | bytes 4621060 | tf_op jit(solution)/shard_map/dot_general | solution.py:84
  45.4 0.1 slice_bitcast_fusion.1
  45.5 0.2 copy.64
  45.8 1.1 %copy.65 = bf16[20,25,8,128]{3,2,0,1:T(8,128)(2,1)} copy(bf16[20,25,8,128]{3,2,1,0:T(8,128)(2,1)S(1)} %get-tuple-element.35) | data formatting | bytes 2048000 | tf_op jit(solution)/shard_map/reshape | solution.py:93
  46.9 2.6 %collective-permute-start = (bf16[200,2560]{1,0:T(8,128)(2,1)}, bf16[200,2560]{1,0:T(8,128)(2,1)}, u32[]{:S(2)}, u32[]{:S(2)}) collective-permute-start(bf16[200,2560]{1,0:T(8,128)(2,1)} %bitcast.69), channel_id=1, source_target_pairs={{0,28},{4,0},{8,4},{12,8},{16,12},{20,16},{24,20},{28,24},{1,29},{... | collective-permute-start | bytes 3072008 | tf_op jit(solution)/shard_map/ppermute | solution.py:18
  49.5 0.3 convert_bitcast_fusion
  49.8 0.8 fusion.23
  50.6 3.8 %slice_reduce_fusion = (f32[400,20]{0,1:T(8,128)S(1)}, f32[400,20]{0,1:T(8,128)S(1)}) fusion(f32[400,20,1,128]{3,0,1,2:T(8,128)S(1)} %convert_bitcast_fusion), kind=kLoop, calls=%fused_computation.7 | loop fusion | bytes 128000 | tf_op jit(solution)/shard_map/slice | solution.py:129
  54.6 0.5 reverse
  55.7 0.2 fusion.11
  55.9 2.7 %copy.52 = f32[400,20,1,1]{3,0,1,2:T(8,128)} copy(f32[400,20,1,1]{0,2,1,3:T(1,128)S(1)} %fusion.11) | data formatting | bytes 64000 | tf_op jit(solution)/shard_map/reshape.57
  59.3 0.5 reverse.1
  59.8 0.2 fusion.12
  60.0 2.7 %copy.53 = f32[400,20,1,1]{3,0,1,2:T(8,128)} copy(f32[400,20,1,1]{0,2,1,3:T(1,128)S(1)} %fusion.12) | data formatting | bytes 64000 | tf_op jit(solution)/shard_map/reshape.68
  62.7 4.7 %fusion.22 = (f32[400,20,1,127]{3,0,1,2:T(8,128)S(1)}, f32[400,20,1,127]{3,0,1,2:T(8,128)S(1)}) fusion(f32[400,20,1,128]{3,0,1,2:T(8,128)} %copy-done.1), kind=kLoop, calls=%fused_computation.60 | loop fusion | bytes 16256000 | tf_op jit(solution)/shard_map/slice | solution.py:118
  67.4 1.1 collective-permute-done.1
  68.5 1.4 %copy_bitcast_fusion.2 = bf16[200,20,128]{2,0,1:T(8,128)(2,1)S(1)} fusion(bf16[200,2560]{1,0:T(8,128)(2,1)} %collective-permute-done.1), kind=kLoop, calls=%fused_computation.20 | loop fusion | bytes 2048000 | tf_op jit(solution)/shard_map/reshape | solution.py:100
  69.9 1.4 %copy_bitcast_fusion.3 = bf16[200,20,128]{2,0,1:T(8,128)(2,1)S(1)} fusion(bf16[200,2560]{1,0:T(8,128)(2,1)} %collective-permute-done), kind=kLoop, calls=%fused_computation.21 | loop fusion | bytes 2048000 | tf_op jit(solution)/shard_map/reshape | solution.py:96
  71.3 3.1 %fusion.4 = f32[400,20,1,128]{3,0,1,2:T(8,128)S(1)} fusion(bf16[400,20,128]{2,0,1:T(8,128)(2,1)S(1)} %add_convert_fusion, f32[400,20,1,127]{3,0,1,2:T(8,128)S(1)} %get-tuple-element.34, f32[400,20,1,127]{3,0,1,2:T(8,128)S(1)} %get-tuple-element.33, f32[20]{0:T(128)S(1)} %get-tuple-element.56, f32[20]{0:T(128)S(1)} %get-tuple-element.57, ...), kind=kLoop, calls=%fused_computation.6 | loop fusion | flops 12288000 | bytes 16355360 | tf_op jit(solution)/shard_map/add | solution.py:122
  74.4 1.9 %copy-done.2 = f32[400,20,1,128]{3,0,1,2:T(8,128)} copy-done((f32[400,20,1,128]{3,0,1,2:T(8,128)}, f32[400,20,1,128]{3,0,1,2:T(8,128)S(1)}, u32[]{:S(2)}) %copy-start.2) | copy-done | bytes 4096024
  76.3 2.4 %slice_add_fusion.1 = f32[400,20,1,1]{3,0,1,2:T(8,128)} fusion(f32[400,20,1,1]{3,0,1,2:T(8,128)S(1)} %copy-done.3, f32[400,20,1,128]{3,0,1,2:T(8,128)S(1)} %fusion.4), kind=kLoop, calls=%fused_computation.11 | loop fusion | flops 8000 | bytes 96000 | tf_op jit(solution)/shard_map/add | solution.py:135
  78.6 8.3 %scatter-add.6 = f32[400,20,1,128]{3,0,1,2:T(8,128)} dynamic-update-slice(f32[400,20,1,128]{3,0,1,2:T(8,128)} %copy-done.2, f32[400,20,1,1]{3,0,1,2:T(8,128)} %slice_add_fusion.1, s32[]{:T(128)} %constant.110.clone.1, s32[]{:T(128)} %constant.110.clone.1, s32[]{:T(128)} %constant.110.clone.1, s32[]{:T(128)} %constant.110.clone.1) | dynamic-update-slice | bytes 64004 | tf_op jit(solution)/shard_map/scatter-add | solution.py:135
  86.9 6.5 %fusion.5 = f32[400,20,1]{2,0,1:T(8,128)} fusion(f32[400,20,1,1]{3,0,1,2:T(8,128)} %copy.53, f32[400,20,1,128]{3,0,1,2:T(8,128)} %scatter-add.6), kind=kLoop, calls=%fused_computation.9 | loop fusion | flops 8000 | bytes 96000 | tf_op jit(solution)/shard_map/reshape | solution.py:137
  93.4 9.9 %scatter-add.9 = f32[400,20,128]{2,0,1:T(8,128)} dynamic-update-slice(f32[400,20,128]{2,0,1:T(8,128)} %bitcast.70, f32[400,20,1]{2,0,1:T(8,128)} %fusion.5, s32[]{:T(128)} %constant.110.clone.1, s32[]{:T(128)} %constant.110.clone.1, s32[]{:T(128)} %constant.114.clone.1) | dynamic-update-slice | bytes 64004 | tf_op jit(solution)/shard_map/scatter-add | solution.py:136
  103.3 3.7 %convert_bitcast_fusion.1 = bf16[1,400,20,128]{3,1,2,0:T(8,128)(2,1)} fusion(f32[400,20,128]{2,0,1:T(8,128)} %scatter-add.9), kind=kLoop, calls=%fused_computation.14 | loop fusion | flops 1024000 | bytes 6144000 | tf_op jit(solution)/shard_map/broadcast_in_dim | solution.py:137
  (47 shorter events, 2.0 us)
Async XLA Ops:
  0.0 37.2 %copy-start = (f32[4,4,13]{2,1,0:T(4,128)S(1)}, f32[4,4,13]{2,1,0:T(4,128)}, u32[]{:S(2)}) copy-start(f32[4,4,13]{2,1,0:T(4,128)} %param.14) | copy-start | bytes 2500
  5.0 7.3 %copy-start.5 = (s32[128]{0:T(128)S(1)}, s32[128]{0:T(128)}, u32[]{:S(2)}) copy-start(s32[128]{0:T(128)} %param.16) | copy-start | bytes 1540
  5.0 7.3 %copy-start.6 = (s32[128]{0:T(128)S(1)}, s32[128]{0:T(128)}, u32[]{:S(2)}) copy-start(s32[128]{0:T(128)} %param.15) | copy-start | bytes 1540
  45.7 22.8 %collective-permute-start.1 = (bf16[200,2560]{1,0:T(8,128)(2,1)S(1)}, bf16[200,2560]{1,0:T(8,128)(2,1)}, u32[]{:S(2)}, u32[]{:S(2)}) collective-permute-start(bf16[200,2560]{1,0:T(8,128)(2,1)S(1)} %bitcast.71), channel_id=1, source_target_pairs={{0,4},{4,8},{8,12},{12,16},{16,20},{20,24},{24,28},{28,0},{1,5},{5... | collective-permute-start | bytes 3072008 | tf_op jit(solution)/shard_map/ppermute | solution.py:18
  45.8 4.1 %copy-start.4 = (s32[2,1]{0,1:T(1,128)S(1)}, s32[2,1]{0,1:T(1,128)}, u32[]{:S(2)}) copy-start(s32[2,1]{0,1:T(1,128)} %param.17) | copy-start | bytes 28
  46.9 23.0 %collective-permute-start = (bf16[200,2560]{1,0:T(8,128)(2,1)}, bf16[200,2560]{1,0:T(8,128)(2,1)}, u32[]{:S(2)}, u32[]{:S(2)}) collective-permute-start(bf16[200,2560]{1,0:T(8,128)(2,1)} %bitcast.69), channel_id=1, source_target_pairs={{0,28},{4,0},{8,4},{12,8},{16,12},{20,16},{24,20},{28,24},{1,29},{... | collective-permute-start | bytes 3072008 | tf_op jit(solution)/shard_map/ppermute | solution.py:18
  49.8 4.6 %copy-start.1 = (f32[400,20,1,128]{3,0,1,2:T(8,128)}, f32[400,20,1,128]{3,0,1,2:T(8,128)S(1)}, u32[]{:S(2)}) copy-start(f32[400,20,1,128]{3,0,1,2:T(8,128)S(1)} %convert_bitcast_fusion) | copy-start | bytes 12288004
  71.3 5.0 %copy-start.3 = (f32[400,20,1,1]{3,0,1,2:T(8,128)S(1)}, f32[400,20,1,1]{3,0,1,2:T(8,128)}, u32[]{:S(2)}) copy-start(f32[400,20,1,1]{3,0,1,2:T(8,128)} %copy.52) | copy-start | bytes 96004
  74.4 1.9 %copy-start.2 = (f32[400,20,1,128]{3,0,1,2:T(8,128)}, f32[400,20,1,128]{3,0,1,2:T(8,128)S(1)}, u32[]{:S(2)}) copy-start(f32[400,20,1,128]{3,0,1,2:T(8,128)S(1)} %fusion.4) | copy-start | bytes 12288004
where the time goes:
time: 109 us; the launch traced here: 107 us
  local copies, waits for them, and re-layouts  55.8 us (51%)
  other arithmetic  18.1 us (17%)
  blocking collectives  14.9 us (14%)
  matrix products  11.4 us (10%)
  between operations  3.03 us (3%)
  starting transfers between devices  2.68 us (2%)
    all_gather x1, blocking collectives, on_device(): lax.all_gather(moments[None], 'species', axis=0, tiled=True)  14.9 us
    scatter-add x1, local copies, waits for them, and re-layouts, on_device(): result = result.at[..., depth_cells - 1].add(top_add)  9.88 us
    scatter-add x1, local copies, waits for them, and re-layouts, on_device(): result = result.at[..., 0].add(bottom_add)  8.28 us
    dot_general x1, matrix products, on_device(): jnp.dot(recon_table.T, cross_terms, precision=lax.Precision.HIGHEST, pref...  8.12 us
    reshape x1, other arithmetic, on_device(): result.reshape(pair_count, node_count, cell_count).astype(jnp.bfloat16)  6.46 us
    dot_general x2, local copies, waits for them, and re-layouts, on_device(): jnp.dot(recon_table.T, cross_terms, precision=lax.Precision.HIGHEST, pref...  5.52 us
    another operation x2, local copies, waits for them, and re-layouts  5.33 us
    unnamed x18, local copies, waits for them, and re-layouts  5.31 us
  transfers between devices with their start and end apart: 2, of which 1 were waited for; matrix products, arithmetic and copies ran while one was open for 18% of the time, Pallas kernels for 0%

commit v1 on v0

v1 whole, which is shorter than its diff:
```python
import math

import numpy as np
import jax
import jax.numpy as jnp
from jax import lax
from jax.sharding import PartitionSpec as P

NZ = 128

courant_max = 0.45
node_reach = 2.85


def passed_along(value, axis, steps):
    count = lax.axis_size(axis)
    pairs = [(source, (source + steps) % count) for source in range(count)]
    return lax.ppermute(value, axis, pairs)


def velocity_tables(node_count):
    pair_count = node_count * node_count
    spacing = 2.0 * node_reach / (node_count - 1)
    node_line = (np.arange(node_count, dtype=np.float64) - 0.5 * (node_count - 1)) * spacing
    grid_shape = (pair_count, node_count)
    along_x = np.broadcast_to(np.repeat(node_line, node_count)[:, None], grid_shape)
    along_y = np.broadcast_to(np.tile(node_line, node_count)[:, None], grid_shape)
    along_z = np.broadcast_to(node_line[None, :], grid_shape)
    square = along_x * along_x + along_y * along_y + along_z * along_z
    heat_term = square - 2.5
    functions = [
        np.ones(grid_shape),
        along_x,
        along_y,
        along_z,
        square - 1.5,
        along_x * along_y,
        along_x * along_z,
        along_y * along_z,
        along_x * along_x - along_y * along_y,
        along_y * along_y - along_z * along_z,
        along_x * heat_term,
        along_y * heat_term,
        along_z * heat_term,
    ]
    stacked = np.stack(functions)
    basis = stacked / np.sqrt(np.mean(stacked * stacked, axis=(1, 2), keepdims=True))
    weights = np.exp(-square) * (spacing * spacing * spacing) / math.pi**1.5
    recon = basis * weights[None]
    return node_line, basis, recon


def bf16_split(table, parts):
    rest = np.asarray(table, np.float64)
    pieces = []
    for _ in range(parts):
        piece = rest.astype(np.float32).astype(jnp.bfloat16).astype(np.float64)
        pieces.append(piece)
        rest = rest - piece
    return pieces


def on_device(cotangent, freq, ratio, coupling, wall, inlet, face_type):
    pair_count = cotangent.shape[1]
    node_count = cotangent.shape[2]
    cell_count = cotangent.shape[3]
    assert cell_count == NZ
    half = pair_count // 2
    moment_count = coupling.shape[2]
    species_count = lax.axis_size("species")

    node_line, basis, recon = velocity_tables(node_count)
    basis_k = np.transpose(basis, (0, 2, 1)).reshape(moment_count, node_count * pair_count)
    basis_parts = np.concatenate(bf16_split(basis_k, 3), axis=0)
    basis_parts = jnp.asarray(basis_parts.astype(jnp.bfloat16))
    recon_k = np.transpose(recon, (0, 2, 1)).astype(np.float32)

    field_in = jnp.transpose(cotangent[0], (1, 0, 2))
    upper_in = field_in[:, half:, :]
    lower_in = field_in[:, :half, :]
    got_next = passed_along(upper_in, "space", -1)
    got_prev = passed_along(lower_in, "space", 1)

    open_cells = (1 - wall).astype(jnp.float32)
    keep_upper = open_cells * (1.0 - inlet.astype(jnp.float32))
    upward = (jnp.arange(pair_count) >= half)[None, :, None]
    keep = jnp.where(upward, keep_upper[None, None, :], open_cells[None, None, :])
    masked = field_in * keep.astype(jnp.bfloat16)
    parts = jnp.dot(
        basis_parts,
        masked.reshape(node_count * pair_count, cell_count),
        preferred_element_type=jnp.float32,
    )
    moments = parts[:moment_count] + parts[moment_count : 2 * moment_count] + parts[2 * moment_count :]

    species_index = lax.axis_index("species")
    row_k = lax.dynamic_index_in_dim(coupling, species_index, axis=0, keepdims=False)
    own_weight = lax.dynamic_index_in_dim(row_k, species_index, axis=0, keepdims=False)
    cross = own_weight[:, None] * moments
    for shift in range(1, species_count):
        source = (species_index - shift) % species_count
        other = passed_along(moments, "species", shift)
        weight = lax.dynamic_index_in_dim(row_k, source, axis=0, keepdims=False)
        cross = cross + weight[:, None] * other

    packet = jnp.concatenate([cross, open_cells[None], keep_upper[None]], axis=0)
    packet_next = passed_along(packet, "space", -1)
    packet_prev = passed_along(packet, "space", 1)

    rate_value = freq[0]
    recon_all = lax.optimization_barrier(jnp.asarray(recon_k))

    def relaxed_of(values, keep_rows, cross_rows, recon_rows):
        rebuilt = jnp.einsum(
            "mnp,mc->npc",
            recon_rows,
            cross_rows,
            precision=lax.Precision.HIGHEST,
            preferred_element_type=jnp.float32,
        )
        return ((1.0 - rate_value) * (values.astype(jnp.float32) * keep_rows) + rebuilt).astype(
            jnp.bfloat16
        ).astype(jnp.float32)

    relaxed = relaxed_of(masked, 1.0, cross, recon_all)
    relaxed_next = relaxed_of(
        got_next,
        packet_next[moment_count + 1][None, None, :],
        packet_next[:moment_count],
        recon_all[:, :, half:],
    )
    relaxed_prev = relaxed_of(
        got_prev,
        packet_prev[moment_count][None, None, :],
        packet_prev[:moment_count],
        recon_all[:, :, :half],
    )

    scale_factor = courant_max * ratio[0] / node_reach
    line = jnp.asarray(node_line.astype(np.float32))
    adv_x = (scale_factor * jnp.repeat(line, node_count))[None, :, None]
    adv_z = (scale_factor * line)[:, None, None]
    plus_x = jnp.maximum(adv_x, 0.0)
    minus_x = jnp.maximum(-adv_x, 0.0)
    plus_z = jnp.maximum(adv_z, 0.0)
    minus_z = jnp.maximum(-adv_z, 0.0)

    shifted_x = jnp.concatenate(
        [minus_x[:, :half] * relaxed_prev, plus_x[:, half:] * relaxed_next], axis=1
    )
    zero_plane = jnp.zeros_like(relaxed[..., :1])
    upper_z = jnp.concatenate([relaxed[..., 1:], zero_plane], axis=2)
    lower_z = jnp.concatenate([zero_plane, relaxed[..., :-1]], axis=2)

    bottom_part = plus_z[::-1, :, 0] * relaxed[::-1, :, 0]
    bottom_add = jnp.where(face_type[0, 0] == 1, bottom_part[:, ::-1], bottom_part)
    top_part = minus_z[::-1, :, 0] * relaxed[::-1, :, NZ - 1]
    top_add = jnp.where(face_type[1, 0] == 1, top_part[:, ::-1], top_part)
    lane = lax.broadcasted_iota(jnp.int32, (1, 1, cell_count), 2)

    result = (1.0 - jnp.abs(adv_x) - jnp.abs(adv_z)) * relaxed
    result = result + shifted_x
    result = result + plus_z * upper_z + minus_z * lower_z
    result = result + jnp.where(lane == 0, bottom_add[:, :, None], 0.0)
    result = result + jnp.where(lane == NZ - 1, top_add[:, :, None], 0.0)
    out = result.astype(jnp.bfloat16)
    return jnp.transpose(out, (1, 0, 2))[None]


def solution(mesh):
    in_specs = (
        P("species", None, None, "space"),
        P("species"),
        P("species"),
        P(),
        P("space"),
        P("space"),
        P(None, "space"),
    )
    out_specs = P("species", None, None, "space")
    return jax.shard_map(
        on_device, mesh=mesh, in_specs=in_specs, out_specs=out_specs, check_vma=False
    )
```

time: 109 us -> 58.6 us (0.54)
  local copies, waits for them, and re-layouts: 55.8 us -> 13.5 us
  blocking collectives: 14.9 us -> 0 us
  starting transfers between devices: 2.68 us -> 11.2 us
  matrix products: 11.4 us -> 16.9 us
  other arithmetic: 18.1 us -> 13.2 us
    scatter-add x2 -> x0, local copies, waits for them, and re-layouts: 18.2 us -> none  [the longest x1 9.88 us: on_device(): result = result.at[..., depth_cells - 1].add(top_add)]
    all_gather x1 -> x0, blocking collectives: 14.9 us -> none  [on_device(): lax.all_gather(moments[None], 'species', axis=0, tiled=True)]
    ppermute x2 -> x7, starting transfers between devices: 2.68 us -> 11.2 us  [passed_along(): return lax.ppermute(value, axis, pairs)]
    another operation x16 -> x1, local copies, waits for them, and re-layouts: 7.42 us -> 0.1 us
    reshape x2 -> x0, other arithmetic: 6.73 us -> none  [the longest x1 6.46 us: on_device(): result.reshape(pair_count, node_count, cell_count).astype(jnp.bfloat16)]
    broadcast_in_dim x1 -> x2, other arithmetic: 3.72 us -> 10.1 us  [the longest x1 9.28 us: on_device(): return jnp.transpose(out, (1, 0, 2))[None]]
    dot_general x2 -> x0, local copies, waits for them, and re-layouts: 5.52 us -> none  [on_device(): jnp.dot(recon_table.T, cross_terms, precision=lax.Precision.HIGHEST, pref...]
    dot_general x2 -> x4, matrix products: 11.4 us -> 16.9 us  [the longest x3 16.4 us: relaxed_of(): jnp.einsum('mnp,mc->npc', recon_rows, cross_rows, precision=lax.Precision...]
  transfers between devices with their start and end apart: 2 -> 7, of which waited for: 1 -> 0; matrix products, arithmetic and copies ran while one was open for 18% -> 43% of each run, Pallas kernels for 0% -> 0%
where the time goes in v1:
time: 58.6 us; the launch traced here: 57.4 us
  matrix products  16.9 us (29%)
  local copies, waits for them, and re-layouts  13.5 us (23%)
  other arithmetic  13.2 us (23%)
  starting transfers between devices  11.2 us (19%)
  between operations  2.77 us (5%)
    dot_general x3, matrix products, relaxed_of(): jnp.einsum('mnp,mc->npc', recon_rows, cross_rows, precision=lax.Precision...  16.4 us
    ppermute x7, starting transfers between devices, passed_along(): return lax.ppermute(value, axis, pairs)  11.2 us
    broadcast_in_dim x1, other arithmetic, on_device(): return jnp.transpose(out, (1, 0, 2))[None]  9.28 us
    slice x1, local copies, waits for them, and re-layouts, on_device(): upper_z = jnp.concatenate([relaxed[..., 1:], zero_plane], axis=2)  4.46 us
    rev x1, local copies, waits for them, and re-layouts, on_device(): top_part = minus_z[::-1, :, 0] * relaxed[::-1, :, NZ - 1]  2.76 us
    mul x1, other arithmetic, on_device(): masked = field_in * keep.astype(jnp.bfloat16)  1.74 us
    slice x1, local copies, waits for them, and re-layouts, on_device(): lower_in = field_in[:, :half, :]  1.5 us
    unnamed x20, local copies, waits for them, and re-layouts  1.35 us
  transfers between devices with their start and end apart: 7, of which 0 were waited for; matrix products, arithmetic and copies ran while one was open for 43% of the time, Pallas kernels for 0%

profile of v1, /device:TPU:0, one launch (start us, length us, event | category | flops | bytes accessed | tf_op | source)
XLA Modules:
  0.0 57.4 jit_solution(11770916029784322469)
XLA Ops:
  0.0 0.8 %fusion.20 = (f32[1,128]{1,0:T(1,128)S(1)}, bf16[128]{0:T(256)(128)(2,1)S(1)}) fusion(s32[128]{0:T(128)} %param.14), kind=kLoop, calls=%fused_computation.55 | loop fusion | flops 384 | bytes 1280 | tf_op jit(solution)/shard_map/broadcast_in_dim | solution.py:106
  0.8 0.7 %subtract_multiply_fusion = f32[128]{0:T(128)S(1)} fusion(s32[128]{0:T(128)} %param.15, s32[128]{0:T(128)} %param.14), kind=kLoop, calls=%fused_computation.50 | loop fusion | flops 640 | bytes 1536 | tf_op jit(solution)/shard_map/mul | solution.py:85
  1.5 0.1 select_convert_fusion
  1.6 1.7 %broadcast_multiply_fusion = bf16[20,400,128]{2,1,0:T(8,128)(2,1)S(1)} fusion(bf16[400,128]{1,0:T(8,128)(2,1)S(1)} %select_convert_fusion, bf16[1,400,20,128]{3,1,2,0:T(8,128)(2,1)} %param.10), kind=kLoop, calls=%fused_computation.15 | loop fusion | flops 1024000 | bytes 4198400 | tf_op jit(solution)/shard_map/mul | solution.py:88
  3.4 0.0 copy-start.6
  3.4 0.0 copy-start.8
  3.4 0.0 copy-start.7
  3.4 0.0 copy-start.3
  3.4 0.5 fusion.25
  4.0 4.1 %collective-permute-start.1 = (f32[13,128]{1,0:T(8,128)S(1)}, f32[13,128]{1,0:T(8,128)S(1)}, u32[]{:S(2)}, u32[]{:S(2)}) collective-permute-start(f32[13,128]{1,0:T(8,128)S(1)} %slice_add_fusion), channel_id=1, source_target_pairs={{0,2},{1,3},{2,0},{3,1},{4,6},{5,7},{6,4},{7,5},{8,10},{9,11},{10,... | collective-permute-start | bytes 19976 | tf_op jit(solution)/shard_map/ppermute | solution.py:18
  8.1 1.6 %collective-permute-start = (f32[13,128]{1,0:T(8,128)S(1)}, f32[13,128]{1,0:T(8,128)S(1)}, u32[]{:S(2)}, u32[]{:S(2)}) collective-permute-start(f32[13,128]{1,0:T(8,128)S(1)} %slice_add_fusion), channel_id=1, source_target_pairs={{0,1},{1,2},{2,3},{3,0},{4,5},{5,6},{6,7},{7,4},{8,9},{9,10},{10,1... | collective-permute-start | bytes 19976 | tf_op jit(solution)/shard_map/ppermute | solution.py:18
  9.7 2.2 %collective-permute-start.2 = (f32[13,128]{1,0:T(8,128)S(1)}, f32[13,128]{1,0:T(8,128)S(1)}, u32[]{:S(2)}, u32[]{:S(2)}) collective-permute-start(f32[13,128]{1,0:T(8,128)S(1)} %slice_add_fusion), channel_id=1, source_target_pairs={{0,3},{1,0},{2,1},{3,2},{4,7},{5,4},{6,5},{7,6},{8,11},{9,8},{10,9... | collective-permute-start | bytes 19976 | tf_op jit(solution)/shard_map/ppermute | solution.py:18
  11.9 1.5 %fusion.23 = (bf16[20,200,128]{2,1,0:T(8,128)(2,1)}, bf16[20,200,128]{2,1,0:T(8,128)(2,1)}) fusion(bf16[20,400,128]{2,1,0:T(8,128)(2,1)S(1)} %bitcast.45), kind=kLoop, calls=%fused_computation.58 | loop fusion | bytes 4096000 | tf_op jit(solution)/shard_map/slice | solution.py:80
  13.4 0.0 collective-permute-start.3
  13.4 2.6 %collective-permute-start.5 = (bf16[20,200,128]{2,1,0:T(8,128)(2,1)}, bf16[20,200,128]{2,1,0:T(8,128)(2,1)}, u32[]{:S(2)}, u32[]{:S(2)}) collective-permute-start(bf16[20,200,128]{2,1,0:T(8,128)(2,1)} %get-tuple-element.10), channel_id=1, source_target_pairs={{0,28},{4,0},{8,4},{12,8},{16,12},{20,16},{24,20},{28,24},{1,29},{... | collective-permute-start | bytes 3072008 | tf_op jit(solution)/shard_map/ppermute | solution.py:18
  16.7 0.6 %fusion.24 = (s32[1,1]{0,1:T(1,128)}, s32[1,1]{0,1:T(1,128)}) fusion(s32[2,1]{0,1:T(1,128)S(1)} %copy-done.6), kind=kLoop, calls=%fused_computation.59 | loop fusion | bytes 16 | tf_op jit(solution)/shard_map/slice | solution.py:156
  17.3 0.1 reverse.10
  17.4 0.1 broadcast_in_dim.83
  17.5 0.1 sub.64
  17.6 0.1 broadcast_subtract_fusion
  17.7 0.8 %fusion.16 = (f32[13]{0:T(128)S(1)}, f32[13]{0:T(128)S(1)}, f32[13]{0:T(128)S(1)}, f32[13]{0:T(128)S(1)}) fusion(f32[4,4,13]{2,1,0:T(4,128)} %param.13, s32[]{:T(128)S(6)} %select_n.70, s32[]{:T(128)S(6)} %select_n.73, s32[]{:T(128)S(6)} %select_n.79, s32[]{:T(128)S(6)} %select_n.76), kind=kLoop, calls=%fused_computation.41 | loop fusion | bytes 432 | tf_op jit(solution)/shard_map/mul | solution.py:99
  20.4 0.1 broadcast_in_dim.87
  20.4 0.1 max.35
  20.6 0.1 broadcast_in_dim.90
  20.6 0.1 max.37
  20.7 0.1 slice.84
  20.8 0.0 collective-permute-done.1
  20.8 0.0 collective-permute-done
  20.8 0.0 collective-permute-done.2
  20.8 0.1 multiply_add_fusion
  20.9 0.1 collective-permute-start.6
  21.0 0.5 collective-permute-start.4
  21.5 6.6 %fusion.6 = f32[20,400,128]{2,1,0:T(8,128)S(1)} fusion(f32[13,20,400]{2,0,1:T(8,128)S(1)} %copy-done.3, bf16[20,400,128]{2,1,0:T(8,128)(2,1)S(1)} %broadcast_multiply_fusion, f32[]{:T(128)} %bitcast.1, f32[13,128]{1,0:T(8,128)S(1)} %multiply_add_fusion), kind=kOutput, calls=%fused_computation.14 | convolution fusion | flops 164864000 | bytes 6566660 | tf_op jit(solution)/shard_map/mnp,mc->npc/dot_general | solution.py:114
  28.1 1.3 %fusion.22 = (f32[20,400,1]{2,1,0:T(8,128)S(1)}, f32[20,400,1]{2,1,0:T(8,128)S(1)}) fusion(f32[20,400,128]{2,1,0:T(8,128)S(1)} %fusion.6), kind=kLoop, calls=%fused_computation.57 | loop fusion | bytes 128000 | tf_op jit(solution)/shard_map/slice | solution.py:155
  29.4 0.6 %copy-done = f32[20,400,128]{2,1,0:T(8,128)} copy-done((f32[20,400,128]{2,1,0:T(8,128)}, f32[20,400,128]{2,1,0:T(8,128)S(1)}, u32[]{:S(2)}) %copy-start) | copy-done | bytes 4096024
  30.0 4.5 %fusion.21 = (f32[20,400,127]{2,1,0:T(8,128)}, f32[20,400,127]{2,1,0:T(8,128)}) fusion(f32[20,400,128]{2,1,0:T(8,128)S(1)} %fusion.6), kind=kLoop, calls=%fused_computation.56 | loop fusion | bytes 16256000 | tf_op jit(solution)/shard_map/slice | solution.py:152
  34.5 2.8 %reverse_reduce_fusion = (f32[20,400]{1,0:T(8,128)S(1)}, f32[20,400]{1,0:T(8,128)S(1)}) fusion(f32[20,400,1]{2,1,0:T(8,128)S(1)} %get-tuple-element.8, f32[20,400,1]{2,1,0:T(8,128)S(1)} %get-tuple-element.7), kind=kLoop, calls=%fused_computation.6 | loop fusion | bytes 128000 | tf_op jit(solution)/shard_map/rev | solution.py:157
  37.2 0.1 broadcast_multiply_fusion.1
  37.3 0.4 reverse.11
  37.7 0.1 broadcast_select_fusion
  37.8 0.1 broadcast_multiply_fusion.2
  37.9 0.3 reverse.12
  38.2 0.1 broadcast_select_fusion.1
  38.3 0.0 collective-permute-done.6
  38.3 0.0 collective-permute-done.3
  38.4 4.9 %convert_multiply_fusion.1 = f32[20,200,128]{2,1,0:T(8,128)S(1)} fusion(bf16[20,200,128]{2,1,0:T(8,128)(2,1)} %collective-permute-done.3, f32[128]{0:T(128)S(1)} %slice_bitcast_fusion.5, f32[]{:T(128)} %bitcast.1, f32[200]{0:T(256)S(1)} %bitcast.48, f32[13,20,400]{2,0,1:T(8,128)S(1)} %copy-done.3, f32[15,128]{1,0:T(8,128)S(1)} %collective-permute-done.4), kind=kOutput, calls=%fused_computation.11 | convolution fusion | flops 83456000 | bytes 3409412 | tf_op jit(solution)/shard_map/mnp,mc->npc/dot_general | solution.py:114
  43.3 4.9 %convert_multiply_fusion = f32[20,200,128]{2,1,0:T(8,128)S(1)} fusion(bf16[20,200,128]{2,1,0:T(8,128)(2,1)} %collective-permute-done.5, f32[128]{0:T(128)S(1)} %slice_bitcast_fusion.4, f32[200]{0:T(256)S(1)} %bitcast.49, f32[]{:T(128)} %bitcast.1, f32[13,20,400]{2,0,1:T(8,128)S(1)} %copy-done.3, f32[15,128]{1,0:T(8,128)S(1)} %collective-permute-done.6), kind=kOutput, calls=%fused_computation.9 | convolution fusion | flops 83456000 | bytes 3409412 | tf_op jit(solution)/shard_map/mnp,mc->npc/dot_general | solution.py:114
  48.1 9.3 %fusion.5 = bf16[1,400,20,128]{3,1,2,0:T(8,128)(2,1)} fusion(f32[20,400]{1,0:T(8,128)S(1)} %broadcast_select_fusion, pred[128]{0:T(512)(128)(4,1)S(1)} %get-tuple-element.26, f32[20,400]{1,0:T(8,128)S(1)} %broadcast_select_fusion.1, pred[128]{0:T(512)(128)(4,1)S(1)} %get-tuple-element.27, f32[20,400,127]{2,1,0:T(8,128)} %get-tuple-element.6, ...), kind=kLoop, calls=%fused_computation.13 | loop fusion | flops 12288000 | bytes 18464416 | tf_op jit(solution)/shard_map/broadcast_in_dim | solution.py:167
  (26 shorter events, 0.1 us)
Async XLA Ops:
  0.0 3.4 %copy-start.4 = (bf16[39,8000]{1,0:T(8,128)(2,1)S(1)}, bf16[39,8000]{1,0:T(8,128)(2,1)}, u32[]{:S(2)}) copy-start(bf16[39,8000]{1,0:T(8,128)(2,1)} %constant.145.clone) | copy-start | bytes 1872004
  0.0 11.9 %copy-start.2 = (bf16[1,400,20,128]{3,1,2,0:T(8,128)(2,1)S(1)}, bf16[1,400,20,128]{3,1,2,0:T(8,128)(2,1)}, u32[]{:S(2)}) copy-start(bf16[1,400,20,128]{3,1,2,0:T(8,128)(2,1)} %param.10) | copy-start | bytes 6144004
  3.4 13.3 %copy-start.6 = (s32[2,1]{0,1:T(1,128)S(1)}, s32[2,1]{0,1:T(1,128)}, u32[]{:S(2)}) copy-start(s32[2,1]{0,1:T(1,128)} %param.16) | copy-start | bytes 28
  3.4 13.9 %copy-start.8 = (f32[20]{0:T(128)S(1)}, f32[20]{0:T(128)}, u32[]{:S(2)}) copy-start(f32[20]{0:T(128)} %constant.156) | copy-start | bytes 244
  3.4 13.9 %copy-start.7 = (f32[20]{0:T(128)S(1)}, f32[20]{0:T(128)}, u32[]{:S(2)}) copy-start(f32[20]{0:T(128)} %constant.147.clone) | copy-start | bytes 244
  3.4 18.1 %copy-start.3 = (f32[13,20,400]{2,0,1:T(8,128)S(1)}, f32[13,20,400]{2,0,1:T(8,128)}, u32[]{:S(2)}) copy-start(f32[13,20,400]{2,0,1:T(8,128)} %constant.146.clone) | copy-start | bytes 1248004
  4.0 16.8 %collective-permute-start.1 = (f32[13,128]{1,0:T(8,128)S(1)}, f32[13,128]{1,0:T(8,128)S(1)}, u32[]{:S(2)}, u32[]{:S(2)}) collective-permute-start(f32[13,128]{1,0:T(8,128)S(1)} %slice_add_fusion), channel_id=1, source_target_pairs={{0,2},{1,3},{2,0},{3,1},{4,6},{5,7},{6,4},{7,5},{8,10},{9,11},{10,... | collective-permute-start | bytes 19976 | tf_op jit(solution)/shard_map/ppermute | solution.py:18
  8.1 12.7 %collective-permute-start = (f32[13,128]{1,0:T(8,128)S(1)}, f32[13,128]{1,0:T(8,128)S(1)}, u32[]{:S(2)}, u32[]{:S(2)}) collective-permute-start(f32[13,128]{1,0:T(8,128)S(1)} %slice_add_fusion), channel_id=1, source_target_pairs={{0,1},{1,2},{2,3},{3,0},{4,5},{5,6},{6,7},{7,4},{8,9},{9,10},{10,1... | collective-permute-start | bytes 19976 | tf_op jit(solution)/shard_map/ppermute | solution.py:18
  9.7 11.1 %collective-permute-start.2 = (f32[13,128]{1,0:T(8,128)S(1)}, f32[13,128]{1,0:T(8,128)S(1)}, u32[]{:S(2)}, u32[]{:S(2)}) collective-permute-start(f32[13,128]{1,0:T(8,128)S(1)} %slice_add_fusion), channel_id=1, source_target_pairs={{0,3},{1,0},{2,1},{3,2},{4,7},{5,4},{6,5},{7,6},{8,11},{9,8},{10,9... | collective-permute-start | bytes 19976 | tf_op jit(solution)/shard_map/ppermute | solution.py:18
  13.4 24.9 %collective-permute-start.3 = (bf16[20,200,128]{2,1,0:T(8,128)(2,1)}, bf16[20,200,128]{2,1,0:T(8,128)(2,1)}, u32[]{:S(2)}, u32[]{:S(2)}) collective-permute-start(bf16[20,200,128]{2,1,0:T(8,128)(2,1)} %get-tuple-element.9), channel_id=1, source_target_pairs={{0,4},{4,8},{8,12},{12,16},{16,20},{20,24},{24,28},{28,0},{1,5},{5... | collective-permute-start | bytes 3072008 | tf_op jit(solution)/shard_map/ppermute | solution.py:18
  13.4 29.8 %collective-permute-start.5 = (bf16[20,200,128]{2,1,0:T(8,128)(2,1)}, bf16[20,200,128]{2,1,0:T(8,128)(2,1)}, u32[]{:S(2)}, u32[]{:S(2)}) collective-permute-start(bf16[20,200,128]{2,1,0:T(8,128)(2,1)} %get-tuple-element.10), channel_id=1, source_target_pairs={{0,28},{4,0},{8,4},{12,8},{16,12},{20,16},{24,20},{28,24},{1,29},{... | collective-permute-start | bytes 3072008 | tf_op jit(solution)/shard_map/ppermute | solution.py:18
  20.5 8.9 %copy-start.5 = (f32[1,400,1]{1,2,0:T(1,128)}, f32[1,400,1]{1,2,0:T(1,128)S(1)}, u32[]{:S(2)}) copy-start(f32[1,400,1]{1,2,0:T(1,128)S(1)} %max.35) | copy-start | bytes 4804
  20.9 17.4 %collective-permute-start.6 = (f32[15,128]{1,0:T(8,128)S(1)}, f32[15,128]{1,0:T(8,128)S(1)}, u32[]{:S(2)}, u32[]{:S(2)}) collective-permute-start(f32[15,128]{1,0:T(8,128)S(1)} %pad_maximum_fusion), channel_id=1, source_target_pairs={{0,28},{4,0},{8,4},{12,8},{16,12},{20,16},{24,20},{28,24},{1,29},{... | collective-permute-start | bytes 23048 | tf_op jit(solution)/shard_map/ppermute | solution.py:18
  21.0 17.3 %collective-permute-start.4 = (f32[15,128]{1,0:T(8,128)S(1)}, f32[15,128]{1,0:T(8,128)S(1)}, u32[]{:S(2)}, u32[]{:S(2)}) collective-permute-start(f32[15,128]{1,0:T(8,128)S(1)} %pad_maximum_fusion), channel_id=1, source_target_pairs={{0,4},{4,8},{8,12},{12,16},{16,20},{20,24},{24,28},{28,0},{1,5},{5... | collective-permute-start | bytes 23048 | tf_op jit(solution)/shard_map/ppermute | solution.py:18
  28.1 1.9 %copy-start = (f32[20,400,128]{2,1,0:T(8,128)}, f32[20,400,128]{2,1,0:T(8,128)S(1)}, u32[]{:S(2)}) copy-start(f32[20,400,128]{2,1,0:T(8,128)S(1)} %fusion.6) | copy-start | bytes 12288004
  34.5 3.9 %slice-start = ((f32[1,400,1]{1,2,0:T(1,128)}), f32[1,200,1]{1,2,0:T(1,128)S(1)}, s32[]{:S(2)}) async-start(f32[1,400,1]{1,2,0:T(1,128)} %copy-done.5), calls=%async_computation | async-start | bytes 2048 | tf_op jit(solution)/shard_map/slice | solution.py:149
  38.2 9.9 %copy-start.1 = (f32[20,400,128]{2,1,0:T(8,128)S(1)}, f32[20,400,128]{2,1,0:T(8,128)}, u32[]{:S(2)}) copy-start(f32[20,400,128]{2,1,0:T(8,128)} %copy-done) | copy-start | bytes 12288004

commit v2 on v1

--- a/solution.py
+++ b/solution.py
@@ -4,6 +4,8 @@
 import jax
 import jax.numpy as jnp
 from jax import lax
+from jax.experimental import pallas as pl
+from jax.experimental.pallas import tpu as pltpu
 from jax.sharding import PartitionSpec as P
 
 NZ = 128
@@ -73,7 +75,7 @@
     basis_k = np.transpose(basis, (0, 2, 1)).reshape(moment_count, node_count * pair_count)
     basis_parts = np.concatenate(bf16_split(basis_k, 3), axis=0)
     basis_parts = jnp.asarray(basis_parts.astype(jnp.bfloat16))
-    recon_k = np.transpose(recon, (0, 2, 1)).astype(np.float32)
+    weight_k = (recon[0] / basis[0]).T.reshape(-1).astype(np.float32)
 
     field_in = jnp.transpose(cotangent[0], (1, 0, 2))
     upper_in = field_in[:, half:, :]
@@ -108,63 +110,150 @@
     packet_prev = passed_along(packet, "space", 1)
 
     rate_value = freq[0]
-    recon_all = lax.optimization_barrier(jnp.asarray(recon_k))
-
-    def relaxed_of(values, keep_rows, cross_rows, recon_rows):
-        rebuilt = jnp.einsum(
-            "mnp,mc->npc",
-            recon_rows,
-            cross_rows,
-            precision=lax.Precision.HIGHEST,
-            preferred_element_type=jnp.float32,
-        )
-        return ((1.0 - rate_value) * (values.astype(jnp.float32) * keep_rows) + rebuilt).astype(
-            jnp.bfloat16
-        ).astype(jnp.float32)
-
-    relaxed = relaxed_of(masked, 1.0, cross, recon_all)
-    relaxed_next = relaxed_of(
-        got_next,
-        packet_next[moment_count + 1][None, None, :],
-        packet_next[:moment_count],
-        recon_all[:, :, half:],
-    )
-    relaxed_prev = relaxed_of(
-        got_prev,
-        packet_prev[moment_count][None, None, :],
-        packet_prev[:moment_count],
-        recon_all[:, :, :half],
-    )
-
     scale_factor = courant_max * ratio[0] / node_reach
     line = jnp.asarray(node_line.astype(np.float32))
-    adv_x = (scale_factor * jnp.repeat(line, node_count))[None, :, None]
-    adv_z = (scale_factor * line)[:, None, None]
-    plus_x = jnp.maximum(adv_x, 0.0)
-    minus_x = jnp.maximum(-adv_x, 0.0)
-    plus_z = jnp.maximum(adv_z, 0.0)
-    minus_z = jnp.maximum(-adv_z, 0.0)
-
-    shifted_x = jnp.concatenate(
-        [minus_x[:, :half] * relaxed_prev, plus_x[:, half:] * relaxed_next], axis=1
-    )
-    zero_plane = jnp.zeros_like(relaxed[..., :1])
-    upper_z = jnp.concatenate([relaxed[..., 1:], zero_plane], axis=2)
-    lower_z = jnp.concatenate([zero_plane, relaxed[..., :-1]], axis=2)
-
-    bottom_part = plus_z[::-1, :, 0] * relaxed[::-1, :, 0]
-    bottom_add = jnp.where(face_type[0, 0] == 1, bottom_part[:, ::-1], bottom_part)
-    top_part = minus_z[::-1, :, 0] * relaxed[::-1, :, NZ - 1]
-    top_add = jnp.where(face_type[1, 0] == 1, top_part[:, ::-1], top_part)
-    lane = lax.broadcasted_iota(jnp.int32, (1, 1, cell_count), 2)
-
-    result = (1.0 - jnp.abs(adv_x) - jnp.abs(adv_z)) * relaxed
-    result = result + shifted_x
-    result = result + plus_z * upper_z + minus_z * lower_z
-    result = result + jnp.where(lane == 0, bottom_add[:, :, None], 0.0)
-    result = result + jnp.where(lane == NZ - 1, top_add[:, :, None], 0.0)
-    out = result.astype(jnp.bfloat16)
+    pair_line = jnp.repeat(line, node_count)
+    adv_x = jnp.abs(scale_factor * pair_line)
+    adv_z = jnp.abs(scale_factor * line)
+    columns = jnp.broadcast_to(
+        jnp.stack([1.0 - adv_x, adv_x])[:, :, None], (2, pair_count, cell_count)
+    )
+    keep_rows = (1.0 - rate_value) * jnp.stack(
+        [open_cells, keep_upper, packet_next[moment_count + 1], packet_prev[moment_count]]
+    )
+    keep_rows = jnp.concatenate([keep_rows, jnp.zeros((4, cell_count), jnp.float32)], axis=0)
+
+    basis_run = lax.optimization_barrier(basis_parts).astype(jnp.float32)
+    basis_sum = (
+        basis_run[:moment_count] + basis_run[moment_count : 2 * moment_count]
+    ) + basis_run[2 * moment_count :]
+    recon_all = (basis_sum * jnp.asarray(weight_k)[None]).reshape(moment_count, node_count, pair_count)
+    r1 = recon_all.astype(jnp.bfloat16)
+    rest = recon_all - r1.astype(jnp.float32)
+    r2 = rest.astype(jnp.bfloat16)
+    r3 = (rest - r2.astype(jnp.float32)).astype(jnp.bfloat16)
+    lanes = 128
+    filler = jnp.zeros((lanes - 6 * moment_count, node_count, pair_count), jnp.bfloat16)
+    recon_parts = jnp.transpose(
+        jnp.concatenate([r1, r1, r2, r1, r2, r3, filler], axis=0), (1, 2, 0)
+    )
+
+    def cross_parts(rows):
+        c1 = rows.astype(jnp.bfloat16)
+        left = rows - c1.astype(jnp.float32)
+        c2 = left.astype(jnp.bfloat16)
+        c3 = (left - c2.astype(jnp.float32)).astype(jnp.bfloat16)
+        pad = jnp.zeros((lanes - 6 * moment_count, cell_count), jnp.bfloat16)
+        return jnp.concatenate([c1, c2, c1, c3, c2, c1, pad], axis=0)
+
+    cross_mats = jnp.stack(
+        [cross_parts(cross), cross_parts(packet_next[:moment_count]), cross_parts(packet_prev[:moment_count])]
+    )
+    flip_rows = lax.broadcasted_iota(jnp.int32, (pair_count, pair_count), 0)
+    flip_cols = lax.broadcasted_iota(jnp.int32, (pair_count, pair_count), 1)
+    flip = (flip_rows + flip_cols == pair_count - 1).astype(jnp.bfloat16)
+    z_weights = jnp.concatenate([adv_z, jnp.zeros((32 - node_count,), jnp.float32)])
+    faces = face_type[:, 0]
+
+    out_lower, out_upper = advect_kernel(
+        field_in, got_next, got_prev, recon_parts, cross_mats, keep_rows, columns, flip, z_weights, faces
+    )
+    out = jnp.concatenate([out_lower, out_upper], axis=0)
     return jnp.transpose(out, (1, 0, 2))[None]
+
+
+def advect_kernel(field_in, got_next, got_prev, recon_parts, cross_mats, keep_rows, columns, flip, z_weights, faces):
+    node_count, pair_count, cell_count = field_in.shape
+    half = pair_count // 2
+    steps = node_count // 2
+
+    def kernel(zw_ref, face_ref, cot_a, cot_b, nxt_a, nxt_b, prv_a, prv_b, rec_a, rec_b,
+               cm_ref, kr_ref, col_ref, flip_ref, out_a, out_b):
+        j = pl.program_id(0)
+        row = lax.broadcasted_iota(jnp.int32, (pair_count, cell_count), 0)
+        lane = lax.broadcasted_iota(jnp.int32, (pair_count, cell_count), 1)
+        kr = kr_ref[...]
+        keep = jnp.where(row >= half, kr[1:2, :], kr[0:1, :])
+        own = cm_ref[0]
+        nxt_m = cm_ref[1]
+        prv_m = cm_ref[2]
+
+        def relax(values, rec, mat, keep_factor):
+            rebuilt = jnp.dot(rec, mat, preferred_element_type=jnp.float32)
+            return (keep_factor * values.astype(jnp.float32) + rebuilt).astype(jnp.bfloat16)
+
+        def halo(nxt, prv, rec):
+            up = jnp.dot(rec, nxt_m, preferred_element_type=jnp.float32)[half:]
+            down = jnp.dot(rec, prv_m, preferred_element_type=jnp.float32)[:half]
+            up = (kr[2:3, :] * nxt.astype(jnp.float32) + up).astype(jnp.bfloat16)
+            down = (kr[3:4, :] * prv.astype(jnp.float32) + down).astype(jnp.bfloat16)
+            return jnp.concatenate([down.astype(jnp.float32), up.astype(jnp.float32)], axis=0)
+
+        rec_a_v = rec_a[0]
+        rec_b_v = rec_b[0]
+        relaxed_a = relax(cot_a[0], rec_a_v, own, keep)
+        relaxed_b = relax(cot_b[0], rec_b_v, own, keep)
+        edges = jnp.where(lane == 0, relaxed_b, relaxed_a)
+        flipped = jnp.dot(flip_ref[...], edges, preferred_element_type=jnp.float32)
+        edges32 = edges.astype(jnp.float32)
+        source_a = jnp.where(face_ref[0] == 1, flipped, edges32)
+        source_b = jnp.where(face_ref[1] == 1, flipped, edges32)
+        ra = relaxed_a.astype(jnp.float32)
+        rb = relaxed_b.astype(jnp.float32)
+        near_a = jnp.where(lane == 0, source_a, pltpu.roll(ra, 1, 1))
+        near_b = jnp.where(lane == cell_count - 1, source_b, pltpu.roll(rb, cell_count - 1, 1))
+        base = col_ref[0]
+        side = col_ref[1]
+        zw_a = zw_ref[j]
+        zw_b = zw_ref[node_count - 1 - j]
+        halo_a = halo(nxt_a[0], prv_a[0], rec_a_v)
+        halo_b = halo(nxt_b[0], prv_b[0], rec_b_v)
+        res_a = (base - zw_a) * ra + side * halo_a
+        res_a = res_a + zw_a * near_a
+        res_b = (base - zw_b) * rb + side * halo_b
+        res_b = res_b + zw_b * near_b
+        out_a[0] = res_a.astype(jnp.bfloat16)
+        out_b[0] = res_b.astype(jnp.bfloat16)
+
+    lower = lambda j: (j, 0, 0)
+    upper = lambda j: (node_count - 1 - j, 0, 0)
+    fixed3 = lambda j: (0, 0, 0)
+    fixed2 = lambda j: (0, 0)
+    slab = (1, pair_count, cell_count)
+    halo_slab = (1, half, cell_count)
+    smem = pl.BlockSpec(memory_space=pltpu.SMEM)
+    in_specs = [
+        smem,
+        smem,
+        pl.BlockSpec(slab, lower),
+        pl.BlockSpec(slab, upper),
+        pl.BlockSpec(halo_slab, lower),
+        pl.BlockSpec(halo_slab, upper),
+        pl.BlockSpec(halo_slab, lower),
+        pl.BlockSpec(halo_slab, upper),
+        pl.BlockSpec(slab, lower),
+        pl.BlockSpec(slab, upper),
+        pl.BlockSpec(cross_mats.shape, fixed3),
+        pl.BlockSpec(keep_rows.shape, fixed2),
+        pl.BlockSpec(columns.shape, fixed3),
+        pl.BlockSpec(flip.shape, fixed2),
+    ]
+    out_specs = [
+        pl.BlockSpec(slab, lambda j: (j, 0, 0)),
+        pl.BlockSpec(slab, lambda j: (steps - 1 - j, 0, 0)),
+    ]
+    out_shape = [
+        jax.ShapeDtypeStruct((steps, pair_count, cell_count), jnp.bfloat16),
+        jax.ShapeDtypeStruct((node_count - steps, pair_count, cell_count), jnp.bfloat16),
+    ]
+    return pl.pallas_call(
+        kernel,
+        grid=(steps,),
+        in_specs=in_specs,
+        out_specs=out_specs,
+        out_shape=out_shape,
+    )(z_weights, faces, field_in, field_in, got_next, got_next, got_prev, got_prev,
+      recon_parts, recon_parts, cross_mats, keep_rows, columns, flip)
 
 
 def solution(mesh):

time: 58.6 us -> 69.2 us (1.18)
  matrix products: 16.9 us -> 0.71 us
  Pallas kernels: 0 us -> 11.2 us
  local copies, waits for them, and re-layouts: 13.5 us -> 23.9 us
  other arithmetic: 13.2 us -> 17.1 us
  waiting for transfers between devices: 0.02 us -> 3.19 us
  between operations: 2.77 us -> 1.47 us
    concatenate x0 -> x6, local copies, waits for them, and re-layouts: none -> 17.6 us  [the longest x1 14.1 us: on_device(): jnp.concatenate([r1, r1, r2, r1, r2, r3, filler], axis=0)]
    dot_general x3 -> x0, matrix products: 16.4 us -> none  [relaxed_of(): jnp.einsum('mnp,mc->npc', recon_rows, cross_rows, precision=lax.Precision...]
    pallas_call x0 -> x1, Pallas kernels: none -> 11.2 us  [advect_kernel(): pl.pallas_call(kernel, grid=(steps,), in_specs=in_specs, out_specs=out_sp...]
    convert_element_type x0 -> x9, other arithmetic: none -> 7.14 us  [the longest x1 2.92 us: on_device(): r3 = (rest - r2.astype(jnp.float32)).astype(jnp.bfloat16)]
    slice x6 -> x2, local copies, waits for them, and re-layouts: 6.42 us -> 0.01 us  [the longest x1 0.01 us: on_device(): packet_next[moment_count + 1]]
    broadcast_in_dim x1, other arithmetic: 9.28 us -> 3 us  [on_device(): return jnp.transpose(out, (1, 0, 2))[None]]
    mul x2, other arithmetic: 0.15 us -> 3.53 us  [the longest x1 3.52 us: on_device(): basis_sum * jnp.asarray(weight_k)[None]]
    ppermute x7, waiting for transfers between devices: 0.02 us -> 3.19 us  [passed_along(): return lax.ppermute(value, axis, pairs)]
  transfers between devices with their start and end apart: 7 -> 7, of which waited for: 0 -> 2; matrix products, arithmetic and copies ran while one was open for 43% -> 47% of each run, Pallas kernels for 0% -> 0%
where the time goes in v2:
time: 69.2 us; the launch traced here: 68.3 us
  local copies, waits for them, and re-layouts  23.9 us (35%)
  other arithmetic  17.1 us (25%)
  Pallas kernels  11.2 us (16%)
  starting transfers between devices  10.8 us (16%)
  waiting for transfers between devices  3.19 us (5%)
  between operations  1.47 us (2%)
  matrix products  0.71 us (1%)
    concatenate x1, local copies, waits for them, and re-layouts, on_device(): jnp.concatenate([r1, r1, r2, r1, r2, r3, filler], axis=0)  14.1 us
    pallas_call x1, Pallas kernels, advect_kernel(): pl.pallas_call(kernel, grid=(steps,), in_specs=in_specs, out_specs=out_sp...  11.2 us
    ppermute x7, starting transfers between devices, passed_along(): return lax.ppermute(value, axis, pairs)  10.8 us
    mul x1, other arithmetic, on_device(): basis_sum * jnp.asarray(weight_k)[None]  3.52 us
    ppermute x7, waiting for transfers between devices, passed_along(): return lax.ppermute(value, axis, pairs)  3.19 us
    broadcast_in_dim x1, other arithmetic, on_device(): return jnp.transpose(out, (1, 0, 2))[None]  3 us
    convert_element_type x1, other arithmetic, on_device(): r3 = (rest - r2.astype(jnp.float32)).astype(jnp.bfloat16)  2.92 us
    convert_element_type x1, other arithmetic, on_device(): r1 = recon_all.astype(jnp.bfloat16)  2.42 us
  transfers between devices with their start and end apart: 7, of which 2 were waited for; matrix products, arithmetic and copies ran while one was open for 47% of the time, Pallas kernels for 0%

profile of v2, /device:TPU:0, one launch (start us, length us, event | category | flops | bytes accessed | tf_op | source)
XLA Modules:
  0.0 68.3 jit_solution(529051033217645937)
XLA Ops:
  0.0 0.7 subtract_convert_fusion.4
  0.7 0.7 subtract_multiply_fusion
  1.3 0.1 select_convert_fusion
  1.5 0.0 copy-start.2
  1.5 1.9 %broadcast_multiply_fusion = bf16[20,400,128]{2,1,0:T(8,128)(2,1)S(1)} fusion(bf16[400,128]{1,0:T(8,128)(2,1)S(1)} %select_convert_fusion, bf16[1,400,20,128]{3,1,2,0:T(8,128)(2,1)} %param.10), kind=kLoop, calls=%fused_computation.7 | loop fusion | flops 1024000 | bytes 4198400 | tf_op jit(solution)/shard_map/mul | solution.py:90
  3.4 0.3 copy-done.2
  3.7 0.7 %fusion.14 = f32[39,128]{1,0:T(8,128)S(1)} fusion(bf16[39,8000]{0,1:T(8,128)(2,1)S(1)} %copy-done.2, bf16[8000,128]{1,0:T(8,128)(2,1)S(1)} %bitcast.37), kind=kOutput, calls=%fused_computation.44 | convolution fusion | flops 79872000 | bytes 2691968 | tf_op jit(solution)/shard_map/dot_general | solution.py:91
  4.4 3.1 %collective-permute-start.2 = (f32[13,128]{1,0:T(8,128)S(1)}, f32[13,128]{1,0:T(8,128)S(1)}, u32[]{:S(2)}, u32[]{:S(2)}) collective-permute-start(f32[13,128]{1,0:T(8,128)S(1)} %slice_add_fusion.2), channel_id=1, source_target_pairs={{0,1},{1,2},{2,3},{3,0},{4,5},{5,6},{6,7},{7,4},{8,9},{9,10},{10,1... | collective-permute-start | bytes 19976 | tf_op jit(solution)/shard_map/ppermute | solution.py:20
  7.5 2.6 %collective-permute-start.3 = (f32[13,128]{1,0:T(8,128)S(1)}, f32[13,128]{1,0:T(8,128)S(1)}, u32[]{:S(2)}, u32[]{:S(2)}) collective-permute-start(f32[13,128]{1,0:T(8,128)S(1)} %slice_add_fusion.2), channel_id=1, source_target_pairs={{0,2},{1,3},{2,0},{3,1},{4,6},{5,7},{6,4},{7,5},{8,10},{9,11},{10,... | collective-permute-start | bytes 19976 | tf_op jit(solution)/shard_map/ppermute | solution.py:20
  10.1 1.3 %collective-permute-start.4 = (f32[13,128]{1,0:T(8,128)S(1)}, f32[13,128]{1,0:T(8,128)S(1)}, u32[]{:S(2)}, u32[]{:S(2)}) collective-permute-start(f32[13,128]{1,0:T(8,128)S(1)} %slice_add_fusion.2), channel_id=1, source_target_pairs={{0,3},{1,0},{2,1},{3,2},{4,7},{5,4},{6,5},{7,6},{8,11},{9,8},{10,9... | collective-permute-start | bytes 19976 | tf_op jit(solution)/shard_map/ppermute | solution.py:20
  11.4 0.0 copy-done.1
  11.4 1.5 %fusion.13 = (bf16[20,200,128]{2,1,0:T(8,128)(2,1)}, bf16[20,200,128]{2,1,0:T(8,128)(2,1)}) fusion(bf16[20,400,128]{2,1,0:T(8,128)(2,1)S(1)} %bitcast.34), kind=kLoop, calls=%fused_computation.43 | loop fusion | bytes 4096000 | tf_op jit(solution)/shard_map/slice | solution.py:82
  13.0 1.0 %collective-permute-start = (bf16[20,200,128]{2,1,0:T(8,128)(2,1)}, bf16[20,200,128]{2,1,0:T(8,128)(2,1)S(1)}, u32[]{:S(2)}, u32[]{:S(2)}) collective-permute-start(bf16[20,200,128]{2,1,0:T(8,128)(2,1)} %get-tuple-element.20), channel_id=1, source_target_pairs={{0,28},{4,0},{8,4},{12,8},{16,12},{20,16},{24,20},{28,24},{1,29},{... | collective-permute-start | bytes 3072008 | tf_op jit(solution)/shard_map/ppermute | solution.py:20
  14.0 0.0 collective-permute-start.1
  14.0 0.8 %fusion.2.flip_ref = bf16[400,400]{1,0:T(8,128)(2,1)} fusion(), kind=kLoop, calls=%fused_computation.9 | loop fusion | flops 480000 | bytes 320000 | tf_op jit(solution)/shard_map/convert_element_type | solution.py:154
  14.8 0.3 convert_element_type.80
  15.1 0.5 copy-done.4
  15.6 3.5 %fusion = f32[13,8000]{0,1:T(8,128)S(1)} fusion(f32[39,8000]{0,1:T(8,128)S(1)} %convert_element_type.80, f32[8000]{0:T(1024)S(1)} %copy-done.4), kind=kLoop, calls=%fused_computation.1 | loop fusion | flops 312000 | bytes 1696000 | tf_op jit(solution)/shard_map/mul | solution.py:130
  19.1 0.0 copy-start
  19.1 0.0 copy-start.5
  19.1 2.9 %subtract_convert_fusion = (bf16[13,20,400]{0,2,1:T(8,128)(2,1)}, bf16[13,20,400]{0,2,1:T(8,128)(2,1)}) fusion(f32[13,20,400]{0,2,1:T(8,128)S(1)} %bitcast.30), kind=kLoop, calls=%fused_computation.3 | loop fusion | flops 728000 | bytes 832000 | tf_op jit(solution)/shard_map/convert_element_type | solution.py:134
  22.0 0.3 copy-done
  23.0 0.0 copy-done.5
  23.0 0.1 broadcast_in_dim.60
  23.1 0.1 abs.20
  23.2 0.8 %fusion.6 = (f32[13]{0:T(128)S(1)}, f32[13]{0:T(128)S(1)}, f32[13]{0:T(128)S(1)}, f32[13]{0:T(128)S(1)}) fusion(f32[4,4,13]{2,1,0:T(4,128)} %param.13, s32[]{:T(128)S(6)} %select_n.48, s32[]{:T(128)S(6)} %select_n.52, s32[]{:T(128)S(6)} %select_n.58, s32[]{:T(128)S(6)} %select_n.55), kind=kLoop, calls=%fused_computation.35 | loop fusion | bytes 432 | tf_op jit(solution)/shard_map/mul | solution.py:101
  24.1 2.4 %convert_element_type.81 = bf16[13,20,400]{0,2,1:T(8,128)(2,1)S(1)} convert(f32[13,20,400]{0,2,1:T(8,128)} %bitcast.31) | non-fusion elementwise | flops 104000 | bytes 624000 | tf_op jit(solution)/shard_map/convert_element_type | solution.py:131
  27.1 0.5 concatenate.24.zw_ref
  27.7 1.6 %broadcast_in_dim.54 = bf16[50,20,400]{0,2,1:T(8,128)(2,1)} broadcast(bf16[]{:T(256)} %constant.129.clone.1), dimensions={} | broadcast | bytes 800002 | tf_op jit(solution)/shard_map/broadcast_in_dim | solution.py:136
  29.2 14.1 %concatenate.25 = bf16[128,20,400]{0,2,1:T(8,128)(2,1)} concatenate(bf16[13,20,400]{0,2,1:T(8,128)(2,1)S(1)} %convert_element_type.81, bf16[13,20,400]{0,2,1:T(8,128)(2,1)S(1)} %convert_element_type.81, bf16[13,20,400]{0,2,1:T(8,128)(2,1)} %get-tuple-element.18, bf16[13,20,400]{0,2,1:T(8,128)(2,1)S(1)} %convert_element_type.81, bf16[13,20,400]{0,2,1:T(8,128)(2,1)} %get-tuple-element.18, ...), dimensions={0} | concatenate | bytes 4096000 | tf_op jit(solution)/shard_map/concatenate | solution.py:138
  43.4 0.0 collective-permute-done.2
  43.4 0.0 collective-permute-done.3
  43.4 0.0 collective-permute-done.4
  43.4 0.1 subtract_convert_fusion.3
  43.5 2.7 %collective-permute-start.5 = (f32[15,128]{1,0:T(8,128)S(1)}, f32[15,128]{1,0:T(8,128)S(1)}, u32[]{:S(2)}, u32[]{:S(2)}) collective-permute-start(f32[15,128]{1,0:T(8,128)S(1)} %pad_maximum_fusion.1), channel_id=1, source_target_pairs={{0,28},{4,0},{8,4},{12,8},{16,12},{20,16},{24,20},{28,24},{1,29},{... | collective-permute-start | bytes 23048 | tf_op jit(solution)/shard_map/ppermute | solution.py:20
  46.2 0.0 collective-permute-start.6
  46.2 0.8 %concatenate.26 = bf16[128,128]{1,0:T(8,128)(2,1)S(1)} concatenate(bf16[13,128]{1,0:T(8,128)(2,1)S(1)} %get-tuple-element.22, bf16[13,128]{1,0:T(8,128)(2,1)S(1)} %get-tuple-element.21, bf16[13,128]{1,0:T(8,128)(2,1)S(1)} %get-tuple-element.22, bf16[13,128]{1,0:T(8,128)(2,1)S(1)} %get-tuple-element.9, bf16[13,128]{1,0:T(8,128)(2,1)S(1)} %get-tuple-element.21, ...), dimensions={0} | concatenate | bytes 65536 | tf_op jit(solution)/shard_map/concatenate | solution.py:147
  47.0 0.6 collective-permute-done.5
  47.5 2.6 %collective-permute-done.6 = f32[15,128]{1,0:T(8,128)S(1)} collective-permute-done((f32[15,128]{1,0:T(8,128)S(1)}, f32[15,128]{1,0:T(8,128)S(1)}, u32[]{:S(2)}, u32[]{:S(2)}) %collective-permute-start.6) | collective-permute-done | bytes 7712 | tf_op jit(solution)/shard_map/ppermute | solution.py:20
  50.2 0.6 concatenate.30.kr_ref
  50.8 0.8 %concatenate.28 = bf16[128,128]{1,0:T(8,128)(2,1)S(1)} concatenate(bf16[13,128]{1,0:T(8,128)(2,1)S(1)} %get-tuple-element.13, bf16[13,128]{1,0:T(8,128)(2,1)S(1)} %get-tuple-element.12, bf16[13,128]{1,0:T(8,128)(2,1)S(1)} %get-tuple-element.13, bf16[13,128]{1,0:T(8,128)(2,1)S(1)} %get-tuple-element.11, bf16[13,128]{1,0:T(8,128)(2,1)S(1)} %get-tuple-element.12, ...), dimensions={0} | concatenate | bytes 65536 | tf_op jit(solution)/shard_map/concatenate | solution.py:147
  51.5 0.8 %concatenate.29 = bf16[128,128]{1,0:T(8,128)(2,1)S(1)} concatenate(bf16[13,128]{1,0:T(8,128)(2,1)S(1)} %get-tuple-element.16, bf16[13,128]{1,0:T(8,128)(2,1)S(1)} %get-tuple-element.15, bf16[13,128]{1,0:T(8,128)(2,1)S(1)} %get-tuple-element.16, bf16[13,128]{1,0:T(8,128)(2,1)S(1)} %get-tuple-element.14, bf16[13,128]{1,0:T(8,128)(2,1)S(1)} %get-tuple-element.15, ...), dimensions={0} | concatenate | bytes 65536 | tf_op jit(solution)/shard_map/concatenate | solution.py:147
  52.3 0.6 pad_maximum_fusion.cm_ref
  53.0 0.0 collective-permute-done.nxt_a.nxt_b
  53.0 0.0 collective-permute-done.1.prv_a.prv_b
  53.0 1.1 %broadcast_in_dim.61.col_ref = f32[2,400,128]{2,1,0:T(8,128)} broadcast(f32[2,400]{1,0:T(2,128)S(1)} %pad_maximum_fusion.2), dimensions={0,1} | broadcast | bytes 412800 | tf_op jit(solution)/shard_map/broadcast_in_dim | solution.py:118
  54.1 11.2 %shard_map.100 = (bf16[10,400,128]{2,1,0:T(8,128)(2,1)}, bf16[10,400,128]{2,1,0:T(8,128)(2,1)}) custom-call(f32[32]{0:T(128)} %concatenate.24.zw_ref, s32[2]{0:T(128)} %bitcast.43, bf16[20,400,128]{2,1,0:T(8,128)(2,1)} %bitcast.32, bf16[20,400,128]{2,1,0:T(8,128)(2,1)} %bitcast.33, bf16[20,200,128]{2,1,0:T(8,128)(2,1)} %copy-done.3, ...), custom_call_target="tpu_custom_call" | custom-call | tf_op jit(solution)/shard_map/pallas_call | solution.py:249
  65.3 3.0 %maximum_bitcast_fusion = bf16[1,400,20,128]{3,1,2,0:T(8,128)(2,1)} fusion(bf16[10,400,128]{2,1,0:T(8,128)(2,1)} %get-tuple-element.8, bf16[10,400,128]{2,1,0:T(8,128)(2,1)} %get-tuple-element.7), kind=kLoop, calls=%fused_computation.6 | loop fusion | flops 1024000 | bytes 4096000 | tf_op jit(solution)/shard_map/broadcast_in_dim | solution.py:162
  (17 shorter events, 0.1 us)
Async XLA Ops:
  1.5 2.2 %copy-start.2 = (bf16[39,8000]{0,1:T(8,128)(2,1)S(1)}, bf16[39,8000]{0,1:T(8,128)(2,1)}, u32[]{:S(2)}) copy-start(bf16[39,8000]{0,1:T(8,128)(2,1)} %constant.142.clone) | copy-start | bytes 1872004
  3.7 7.8 %copy-start.1 = (bf16[1,400,20,128]{3,1,2,0:T(8,128)(2,1)S(1)}, bf16[1,400,20,128]{3,1,2,0:T(8,128)(2,1)}, u32[]{:S(2)}) copy-start(bf16[1,400,20,128]{3,1,2,0:T(8,128)(2,1)} %param.10) | copy-start | bytes 6144004
  4.4 39.0 %collective-permute-start.2 = (f32[13,128]{1,0:T(8,128)S(1)}, f32[13,128]{1,0:T(8,128)S(1)}, u32[]{:S(2)}, u32[]{:S(2)}) collective-permute-start(f32[13,128]{1,0:T(8,128)S(1)} %slice_add_fusion.2), channel_id=1, source_target_pairs={{0,1},{1,2},{2,3},{3,0},{4,5},{5,6},{6,7},{7,4},{8,9},{9,10},{10,1... | collective-permute-start | bytes 19976 | tf_op jit(solution)/shard_map/ppermute | solution.py:20
  7.5 35.9 %collective-permute-start.3 = (f32[13,128]{1,0:T(8,128)S(1)}, f32[13,128]{1,0:T(8,128)S(1)}, u32[]{:S(2)}, u32[]{:S(2)}) collective-permute-start(f32[13,128]{1,0:T(8,128)S(1)} %slice_add_fusion.2), channel_id=1, source_target_pairs={{0,2},{1,3},{2,0},{3,1},{4,6},{5,7},{6,4},{7,5},{8,10},{9,11},{10,... | collective-permute-start | bytes 19976 | tf_op jit(solution)/shard_map/ppermute | solution.py:20
  10.1 33.3 %collective-permute-start.4 = (f32[13,128]{1,0:T(8,128)S(1)}, f32[13,128]{1,0:T(8,128)S(1)}, u32[]{:S(2)}, u32[]{:S(2)}) collective-permute-start(f32[13,128]{1,0:T(8,128)S(1)} %slice_add_fusion.2), channel_id=1, source_target_pairs={{0,3},{1,0},{2,1},{3,2},{4,7},{5,4},{6,5},{7,6},{8,11},{9,8},{10,9... | collective-permute-start | bytes 19976 | tf_op jit(solution)/shard_map/ppermute | solution.py:20
  13.0 40.0 %collective-permute-start = (bf16[20,200,128]{2,1,0:T(8,128)(2,1)}, bf16[20,200,128]{2,1,0:T(8,128)(2,1)S(1)}, u32[]{:S(2)}, u32[]{:S(2)}) collective-permute-start(bf16[20,200,128]{2,1,0:T(8,128)(2,1)} %get-tuple-element.20), channel_id=1, source_target_pairs={{0,28},{4,0},{8,4},{12,8},{16,12},{20,16},{24,20},{28,24},{1,29},{... | collective-permute-start | bytes 3072008 | tf_op jit(solution)/shard_map/ppermute | solution.py:20
  14.0 39.0 %collective-permute-start.1 = (bf16[20,200,128]{2,1,0:T(8,128)(2,1)}, bf16[20,200,128]{2,1,0:T(8,128)(2,1)}, u32[]{:S(2)}, u32[]{:S(2)}) collective-permute-start(bf16[20,200,128]{2,1,0:T(8,128)(2,1)} %get-tuple-element.19), channel_id=1, source_target_pairs={{0,4},{4,8},{8,12},{12,16},{16,20},{20,24},{24,28},{28,0},{1,5},{5... | collective-permute-start | bytes 3072008 | tf_op jit(solution)/shard_map/ppermute | solution.py:20
  14.8 0.8 %copy-start.4 = (f32[8000]{0:T(1024)S(1)}, f32[8000]{0:T(1024)}, u32[]{:S(2)}) copy-start(f32[8000]{0:T(1024)} %constant.144.clone) | copy-start | bytes 96004
  19.1 3.3 %copy-start = (f32[13,8000]{0,1:T(8,128)}, f32[13,8000]{0,1:T(8,128)S(1)}, u32[]{:S(2)}) copy-start(f32[13,8000]{0,1:T(8,128)S(1)} %fusion) | copy-start | bytes 1248004
  19.1 3.9 %copy-start.5 = (f32[20]{0:T(128)S(1)}, f32[20]{0:T(128)}, u32[]{:S(2)}) copy-start(f32[20]{0:T(128)} %constant.143.clone) | copy-start | bytes 244
  43.5 4.1 %collective-permute-start.5 = (f32[15,128]{1,0:T(8,128)S(1)}, f32[15,128]{1,0:T(8,128)S(1)}, u32[]{:S(2)}, u32[]{:S(2)}) collective-permute-start(f32[15,128]{1,0:T(8,128)S(1)} %pad_maximum_fusion.1), channel_id=1, source_target_pairs={{0,28},{4,0},{8,4},{12,8},{16,12},{20,16},{24,20},{28,24},{1,29},{... | collective-permute-start | bytes 23048 | tf_op jit(solution)/shard_map/ppermute | solution.py:20
  46.2 4.0 %collective-permute-start.6 = (f32[15,128]{1,0:T(8,128)S(1)}, f32[15,128]{1,0:T(8,128)S(1)}, u32[]{:S(2)}, u32[]{:S(2)}) collective-permute-start(f32[15,128]{1,0:T(8,128)S(1)} %pad_maximum_fusion.1), channel_id=1, source_target_pairs={{0,4},{4,8},{8,12},{12,16},{16,20},{20,24},{24,28},{28,0},{1,5},{5... | collective-permute-start | bytes 23048 | tf_op jit(solution)/shard_map/ppermute | solution.py:20
  53.0 1.1 %copy-start.3 = (bf16[20,200,128]{2,1,0:T(8,128)(2,1)}, bf16[20,200,128]{2,1,0:T(8,128)(2,1)S(1)}, u32[]{:S(2)}) copy-start(bf16[20,200,128]{2,1,0:T(8,128)(2,1)S(1)} %collective-permute-done.nxt_a.nxt_b) | copy-start | bytes 3072004
